TPU v7x, 32 devices: a whole 2x2x4 slice. The times are simulated.
32 devices in a mesh: dp: 4 (over x, core), seq: 8 (over z, y).
Axes of the slice: x: 2, y: 2, z: 4, core: 2. Of those that a mesh axis runs over, the one named last changes fastest.
Arguments:
- queries: bfloat16 [4, 4096, 2048], P('dp', 'seq'), may hold values from -34 to 34
- neighbour_input: bfloat16 [4, 32, 64, 896], P('dp', 'seq'), may hold values from -6 to 6
- owner_list: int32 [4, 64, 2], P('dp', 'seq'), may hold values from 0 to 7, as said below
- block_list: int32 [4, 64, 2], P('dp', 'seq'), may hold values from 0 to 3
- enc_gain: float32 [896], replicated, may hold values from 0.5 to 8
- enc_attn: bfloat16 [4, 896, 896], P(None, 'dp'), may hold values from -0.1875 to 0.1875
- kv_weight: bfloat16 [2, 896, 2048], replicated, may hold values from -0.1875 to 0.1875
Outputs:
- context: bfloat16 [4, 4096, 2048], P('dp', 'seq')
Inputs may be any that keep to these rules, and one draw needn't show every extreme that they name: `owner_list`: within the spans of one device, no owner is named more than 2 times; every owner is named in every sequence.
All inputs are finite; a program needn't handle non-finite values.
Results may differ from a plain program's by a relative error of at most 0.025.
The roundings to bfloat16 on the way count: a program that leaves them out, or rounds other values in their place, can miss the bound.
Values may be sent and summed in bfloat16 or wider, within the bound.
No kernel may reach another device: no remote copies, remote signals or barrier semaphores. Data moves between devices by JAX's collectives and lax.ppermute only.
A program may use at most 128 MiB of HBM per device.

v0:
```python
import jax
import jax.numpy as jnp
from jax import lax
from jax.sharding import PartitionSpec as P

HEADS = 16
HEAD_DIM = 128
ENC_HEADS = 7
NLEN = 64
SPAN = 64
NEIGH = 2
NB_DEV = 4
epsilon = 1e-05


def softmax_rows(scores):
    highest = jnp.max(scores, axis=-1, keepdims=True)
    raised = jnp.exp(scores - highest)
    return raised / jnp.sum(raised, axis=-1, keepdims=True)


def encode(blocks, gain, attention):
    inputs = blocks.astype(jnp.float32)
    spread = jnp.mean(inputs * inputs, axis=-1, keepdims=True)
    normed = (inputs * lax.rsqrt(spread + epsilon) * gain).astype(jnp.bfloat16)
    count, length, width = blocks.shape
    head_size = width // ENC_HEADS
    projected = jnp.einsum(
        "nte,pef->pntf", normed, attention[:3], preferred_element_type=jnp.float32
    ).astype(jnp.bfloat16)
    split_heads = projected.reshape(3, count, length, ENC_HEADS, head_size)
    scores = jnp.einsum(
        "nqhd,nkhd->nhqk", split_heads[0], split_heads[1], preferred_element_type=jnp.float32
    ) * head_size ** (-0.5)
    weights = softmax_rows(scores).astype(jnp.bfloat16)
    mixture = jnp.einsum(
        "nhqk,nkhd->nqhd", weights, split_heads[2], preferred_element_type=jnp.float32
    ).astype(jnp.bfloat16)
    mixture = mixture.reshape(count, length, width)
    output = jnp.einsum("nte,ef->ntf", mixture, attention[3], preferred_element_type=jnp.float32)
    return (inputs + output).astype(jnp.bfloat16)


def shards(queries, neighbour_input, owner_list, block_list, enc_gain, enc_attn, kv_weight):
    full_weights = lax.all_gather(enc_attn, "dp", axis=1, tiled=True)
    encoded = encode(neighbour_input[0], enc_gain, full_weights)
    owners = owner_list.reshape(-1)
    indices = block_list.reshape(-1)
    global_ids = owners * NB_DEV + indices
    piece = lax.all_gather(encoded, "seq", axis=0, tiled=True)
    selector = (global_ids[:, None] == jnp.arange(piece.shape[0], dtype=jnp.int32)[None, :]).astype(
        jnp.bfloat16
    )
    chosen = jnp.einsum("rb,bte->rte", selector, piece, preferred_element_type=jnp.float32).astype(
        jnp.bfloat16
    )
    key_value = jnp.einsum(
        "rte,pef->prtf", chosen, kv_weight, preferred_element_type=jnp.float32
    ).astype(jnp.bfloat16)
    span_count = queries.shape[1] // SPAN
    memory_keys = key_value[0].reshape(span_count, NEIGH * NLEN, HEADS, HEAD_DIM)
    memory_values = key_value[1].reshape(span_count, NEIGH * NLEN, HEADS, HEAD_DIM)
    grouped = queries[0].reshape(span_count, SPAN, HEADS, HEAD_DIM)
    scores = jnp.einsum(
        "cqhd,ckhd->chqk", grouped, memory_keys, preferred_element_type=jnp.float32
    ) * HEAD_DIM ** (-0.5)
    weights = softmax_rows(scores).astype(jnp.bfloat16)
    mixture = jnp.einsum(
        "chqk,ckhd->cqhd", weights, memory_values, preferred_element_type=jnp.float32
    ).astype(jnp.bfloat16)
    return mixture.reshape(queries.shape)


def solution(mesh):
    return jax.shard_map(
        shards,
        mesh=mesh,
        in_specs=(
            P("dp", "seq", None),
            P("dp", "seq", None, None),
            P("dp", "seq", None),
            P("dp", "seq", None),
            P(),
            P(None, "dp", None),
            P(),
        ),
        out_specs=P("dp", "seq", None),
        check_vma=False,
    )
```

profile of v0, /device:TPU:0, one launch (start us, length us, event | category | flops | bytes accessed | tf_op | source)
XLA Modules:
  0.0 194.3 jit_solution(1259733458802943780)
XLA Ops:
  6.5 0.7 all-gather.3.cloned.1.call-update
  7.3 1.2 fusion.33
  8.5 50.3 %all-gather.3.cloned.1.call-done = bf16[4,896,896]{2,1,0:T(8,128)(2,1)} async-done(((bf16[4,224,896]{2,1,0:T(8,128)(2,1)}), bf16[4,896,896]{2,1,0:T(8,128)(2,1)}) %all-gather.3.cloned.1.call-update) | async-done | bytes 6422544 | tf_op jit(solution)/shard_map/all_gather | solution.py:45
  58.8 4.3 %fusion.28 = bf16[3,4,64,896]{3,2,0,1:T(8,128)(2,1)S(1)} fusion(bf16[4,896,896]{2,1,0:T(8,128)(2,1)} %all-gather.3.cloned.1.call-done, bf16[1,4,64,896]{3,2,1,0:T(8,128)(2,1)} %param.8, f32[896]{0:T(1024)} %param.11, f32[4,64]{1,0:T(4,128)S(1)} %add_rsqrt_fusion), kind=kOutput, calls=%fused_computation.28 | convolution fusion | flops 1234731008 | bytes 6657024 | tf_op jit(solution)/shard_map/nte,pef->pntf/dot_general | solution.py:28
  63.0 0.1 fusion.65
  63.2 0.5 squeeze.14
  63.7 0.5 squeeze.15
  64.2 0.4 convolution_multiply_fusion
  64.6 0.5 fusion.66
  65.1 0.5 squeeze.13
  65.6 0.4 fusion.32
  66.1 2.9 %fusion.31 = bf16[4,64,896]{2,1,0:T(8,128)(2,1)} fusion(bf16[4,896,896]{2,1,0:T(8,128)(2,1)} %all-gather.3.cloned.1.call-done, bf16[4,7,8,8,128]{4,3,2,1,0:T(8,128)(2,1)S(1)} %fusion.32, bf16[1,4,64,896]{3,2,1,0:T(8,128)(2,1)S(1)} %copy-done.1), kind=kOutput, calls=%fused_computation.36 | convolution fusion | flops 411729920 | bytes 2981888 | tf_op jit(solution)/shard_map/nte,ef->ntf/dot_general | solution.py:40
  69.2 2.2 %copy.45 = bf16[64,8,16,128]{3,2,1,0:T(8,128)(2,1)S(1)} copy(bf16[64,8,16,128]{3,1,2,0:T(8,128)(2,1)} %bitcast.105) | data formatting | bytes 4194304
  71.4 64.6 %all-gather.5.cloned.1.call-done = bf16[32,64,896]{2,1,0:T(8,128)(2,1)} async-done(((bf16[4,64,896]{2,1,0:T(8,128)(2,1)}), bf16[32,64,896]{2,1,0:T(8,128)(2,1)}) %all-gather.5.cloned.1.call-update) | async-done | bytes 3670032 | tf_op jit(solution)/shard_map/all_gather | solution.py:50
  136.0 5.0 %convert_bitcast_fusion.2 = bf16[16,64,896,1]{2,0,1,3:T(8,128)(2,1)S(1)} fusion(bf16[32,64,896]{2,1,0:T(8,128)(2,1)} %all-gather.5.cloned.1.call-done, s32[16]{0:T(128)S(1)} %add.25), kind=kOutput, calls=%fused_computation.24 | convolution fusion | flops 59638272 | bytes 5505088 | tf_op jit(solution)/shard_map/rb,bte->rte/dot_general | solution.py:54
  141.0 11.3 %convert_bitcast_fusion = bf16[2,16,64,2048]{3,2,0,1:T(8,128)(2,1)S(1)} fusion(bf16[2,896,2048]{2,1,0:T(8,128)(2,1)} %param.13, bf16[16,64,896,1]{2,0,1,3:T(8,128)(2,1)S(1)} %convert_bitcast_fusion.2), kind=kOutput, calls=%fused_computation.2 | convolution fusion | flops 7520387072 | bytes 17563648 | tf_op jit(solution)/shard_map/rte,pef->prtf/dot_general | solution.py:57
  152.3 1.2 fusion.64
  153.5 1.4 copy.44
  154.9 3.0 %fusion.11 = f32[8,16,128,64]{2,3,1,0:T(8,128)S(1)} fusion(bf16[8,128,16,128]{3,2,1,0:T(8,128)(2,1)S(1)} %bitcast.100, bf16[8,64,16,128]{3,2,1,0:T(8,128)(2,1)S(1)} %bitcast.103), kind=kOutput, calls=%fused_computation.13 | convolution fusion | flops 268435456 | bytes 10485760 | tf_op jit(solution)/shard_map/cqhd,ckhd->chqk/dot_general | solution.py:64
  157.9 2.2 %fusion.71 = f32[8,16,64]{2,1,0:T(8,128)S(1)} fusion(f32[8,16,128,64]{2,3,1,0:T(8,128)S(1)} %fusion.11), kind=kOutput, calls=%fused_computation.65 | output fusion | flops 4194431 | bytes 4227072 | tf_op jit(solution)/shard_map/sub | solution.py:18
  160.1 3.3 %copy.46 = bf16[128,8,16,128]{3,2,1,0:T(8,128)(2,1)} copy(bf16[128,8,16,128]{3,1,2,0:T(8,128)(2,1)S(1)} %bitcast.101) | data formatting | bytes 8388608
  163.4 18.7 %convert_bitcast_fusion.1 = bf16[8,64,16,128]{3,1,2,0:T(8,128)(2,1)} fusion(bf16[8,128,16,128]{3,2,1,0:T(8,128)(2,1)} %bitcast.104, f32[8,16,64]{2,1,0:T(8,128)S(1)} %fusion.71, f32[8,16,128,64]{2,3,1,0:T(8,128)} %copy-done), kind=kOutput, calls=%fused_computation.20 | convolution fusion | flops 274735232 | bytes 10518528 | tf_op jit(solution)/shard_map/chqk,ckhd->cqhd/dot_general | solution.py:68
  182.2 3.0 %copy.37 = bf16[8,64,16,128]{3,2,1,0:T(8,128)(2,1)S(1)} copy(bf16[8,64,16,128]{3,1,2,0:T(8,128)(2,1)} %convert_bitcast_fusion.1) | data formatting | bytes 4194304 | tf_op jit(solution)/shard_map/convert_element_type | solution.py:70
  185.1 2.3 %reshape.44 = bf16[1,512,2048]{2,1,0:T(8,128)(2,1)} reshape(bf16[8,64,16,128]{3,2,1,0:T(8,128)(2,1)S(1)} %copy.37) | data formatting | bytes 4194304 | tf_op jit(solution)/shard_map/reshape | solution.py:71
  (15 shorter events, 0.3 us)
Async XLA Ops:
  6.5 52.2 %all-gather.3.cloned.1.call-start = ((), (), s32[]{:S(2)}) async-start(), calls=%async_computation | async-start | bytes 8028160 | tf_op jit(solution)/shard_map/all_gather | solution.py:45
  7.3 128.7 %all-gather.5.cloned.1.call-start = ((), (), s32[]{:S(2)}) async-start(), calls=%async_computation.1 | async-start | bytes 4128768 | tf_op jit(solution)/shard_map/all_gather | solution.py:50
  64.6 1.5 copy-start.1
  65.6 3.4 %copy-start.2 = (s32[1,8,2]{1,2,0:T(2,128)S(1)}, s32[1,8,2]{1,2,0:T(2,128)}, u32[]{:S(2)}) copy-start(s32[1,8,2]{1,2,0:T(2,128)} %param.10) | copy-start | bytes 196
  65.6 3.4 %copy-start.3 = (s32[1,8,2]{1,2,0:T(2,128)S(1)}, s32[1,8,2]{1,2,0:T(2,128)}, u32[]{:S(2)}) copy-start(s32[1,8,2]{1,2,0:T(2,128)} %param.9) | copy-start | bytes 196
  157.9 5.6 %copy-start = (f32[8,16,128,64]{2,3,1,0:T(8,128)}, f32[8,16,128,64]{2,3,1,0:T(8,128)S(1)}, u32[]{:S(2)}) copy-start(f32[8,16,128,64]{2,3,1,0:T(8,128)S(1)} %fusion.11) | copy-start | bytes 12582916
Sparse Core Ops, SparseCore 0:
  8.9 49.8 all-gather.2
  69.1 66.8 all-gather.4
where the time goes:
time: 195 us; the launch traced here: 194 us
  waiting for transfers between devices  116 us (59%)
  matrix products  46.4 us (24%)
  local copies, waits for them, and re-layouts  15.3 us (8%)
  between operations  13.5 us (7%)
  other arithmetic  3.45 us (2%)
    all_gather x1, waiting for transfers between devices, shards(): piece = lax.all_gather(encoded, 'seq', axis=0, tiled=True)  64.6 us
    all_gather x1, waiting for transfers between devices, shards(): full_weights = lax.all_gather(enc_attn, 'dp', axis=1, tiled=True)  50.3 us
    dot_general x1, matrix products, shards(): jnp.einsum('chqk,ckhd->cqhd', weights, memory_values, preferred_element_t...  18.7 us
    dot_general x1, matrix products, shards(): jnp.einsum('rte,pef->prtf', chosen, kv_weight, preferred_element_type=jnp...  11.3 us
    unnamed x11, local copies, waits for them, and re-layouts  6.96 us
    dot_general x1, matrix products, shards(): jnp.einsum('rb,bte->rte', selector, piece, preferred_element_type=jnp.flo...  5.01 us
    dot_general x1, matrix products, encode(): jnp.einsum('nte,pef->pntf', normed, attention[:3], preferred_element_type...  4.25 us
  transfers between devices with their start and end apart: 2, of which 2 were waited for; matrix products, arithmetic and copies ran while one was open for 2% of the time, Pallas kernels for 0%

commit v1 on v0

--- a/solution.py
+++ b/solution.py
@@ -11,6 +11,16 @@
 NEIGH = 2
 NB_DEV = 4
 epsilon = 1e-05
+
+
+def turned_line(value, mesh_axis, along):
+    size = lax.axis_size(mesh_axis)
+    held, blocks = (value, [value])
+    for _ in range(size - 1):
+        held = lax.ppermute(held, mesh_axis, [(i, (i + 1) % size) for i in range(size)])
+        blocks.insert(0, held)
+    line = jnp.concatenate(blocks, axis=along)
+    return jnp.roll(line, (lax.axis_index(mesh_axis) + 1) * value.shape[along], axis=along)
 
 
 def softmax_rows(scores):
@@ -47,7 +57,7 @@
     owners = owner_list.reshape(-1)
     indices = block_list.reshape(-1)
     global_ids = owners * NB_DEV + indices
-    piece = lax.all_gather(encoded, "seq", axis=0, tiled=True)
+    piece = turned_line(encoded, "seq", 0)
     selector = (global_ids[:, None] == jnp.arange(piece.shape[0], dtype=jnp.int32)[None, :]).astype(
         jnp.bfloat16
     )

time: 195 us -> 225 us (1.15)
  waiting for transfers between devices: 116 us -> 138 us
  local copies, waits for them, and re-layouts: 15.3 us -> 26 us
  matrix products: 46.4 us -> 41.9 us
    ppermute x0 -> x7, waiting for transfers between devices: none -> 87 us  [turned_line(): lax.ppermute(held, mesh_axis, [(i, (i + 1) % size) for i in range(size)])]
    all_gather x1 -> x0, waiting for transfers between devices: 64.6 us -> none  [shards(): piece = lax.all_gather(encoded, 'seq', axis=0, tiled=True)]
    unnamed x11 -> x42, local copies, waits for them, and re-layouts: 6.96 us -> 17.3 us
  transfers between devices with their start and end apart: 2 -> 8, of which waited for: 2 -> 8; matrix products, arithmetic and copies ran while one was open for 2% -> 2% of each run, Pallas kernels for 0% -> 0%
where the time goes in v1:
time: 225 us
  waiting for transfers between devices  138 us (61%)
  matrix products  41.9 us (19%)
  local copies, waits for them, and re-layouts  26 us (12%)
  between operations  13.7 us (6%)
  other arithmetic  3.45 us (2%)
    ppermute x7, waiting for transfers between devices, turned_line(): lax.ppermute(held, mesh_axis, [(i, (i + 1) % size) for i in range(size)])  87 us
    all_gather x1, waiting for transfers between devices, shards(): full_weights = lax.all_gather(enc_attn, 'dp', axis=1, tiled=True)  50.3 us
    dot_general x1, matrix products, shards(): jnp.einsum('chqk,ckhd->cqhd', weights, memory_values, preferred_element_t...  18.6 us
    unnamed x42, local copies, waits for them, and re-layouts  17.3 us
    dot_general x1, matrix products, shards(): jnp.einsum('rte,pef->prtf', chosen, kv_weight, preferred_element_type=jnp...  9.67 us
  transfers between devices with their start and end apart: 8, of which 8 were waited for; matrix products, arithmetic and copies ran while one was open for 2% of the time, Pallas kernels for 0%

profile of v1, /device:TPU:0, one launch (start us, length us, event | category | flops | bytes accessed | tf_op | source)
XLA Modules:
  0.0 224.7 jit_solution(9346381169135983148)
XLA Ops:
  7.3 1.2 fusion.32
  8.5 50.3 %all-gather.2.cloned.1.call-done = bf16[4,896,896]{2,1,0:T(8,128)(2,1)} async-done(((bf16[4,224,896]{2,1,0:T(8,128)(2,1)}), bf16[4,896,896]{2,1,0:T(8,128)(2,1)}) %all-gather.2.cloned.1.call-update) | async-done | bytes 6422544 | tf_op jit(solution)/shard_map/all_gather | solution.py:55
  58.8 4.3 %fusion.27 = bf16[3,4,64,896]{3,2,0,1:T(8,128)(2,1)S(1)} fusion(bf16[4,896,896]{2,1,0:T(8,128)(2,1)} %all-gather.2.cloned.1.call-done, bf16[1,4,64,896]{3,2,1,0:T(8,128)(2,1)} %param.8, f32[896]{0:T(1024)} %param.11, f32[4,64]{1,0:T(4,128)S(1)} %add_rsqrt_fusion), kind=kOutput, calls=%fused_computation.28 | convolution fusion | flops 1234731008 | bytes 6657024 | tf_op jit(solution)/shard_map/nte,pef->pntf/dot_general | solution.py:38
  66.1 2.1 fusion.30
  68.2 1.5 collective-permute-start
  69.7 13.9 %collective-permute-done = bf16[4,64,896]{2,1,0:T(8,128)(2,1)S(1)} collective-permute-done((bf16[4,64,896]{2,1,0:T(8,128)(2,1)S(1)}, bf16[4,64,896]{2,1,0:T(8,128)(2,1)S(1)}, u32[]{:S(2)}, u32[]{:S(2)}) %collective-permute-start) | collective-permute-done | bytes 458784 | tf_op jit(solution)/shard_map/ppermute | solution.py:20
  83.6 14.6 %collective-permute-done.1 = bf16[4,64,896]{2,1,0:T(8,128)(2,1)S(1)} collective-permute-done((bf16[4,64,896]{2,1,0:T(8,128)(2,1)S(1)}, bf16[4,64,896]{2,1,0:T(8,128)(2,1)S(1)}, u32[]{:S(2)}, u32[]{:S(2)}) %collective-permute-start.1) | collective-permute-done | bytes 458784 | tf_op jit(solution)/shard_map/ppermute | solution.py:20
  98.2 13.6 %collective-permute-done.2 = bf16[4,64,896]{2,1,0:T(8,128)(2,1)S(1)} collective-permute-done((bf16[4,64,896]{2,1,0:T(8,128)(2,1)S(1)}, bf16[4,64,896]{2,1,0:T(8,128)(2,1)S(1)}, u32[]{:S(2)}, u32[]{:S(2)}) %collective-permute-start.2) | collective-permute-done | bytes 458784 | tf_op jit(solution)/shard_map/ppermute | solution.py:20
  112.6 12.7 %collective-permute-done.3 = bf16[4,64,896]{2,1,0:T(8,128)(2,1)S(1)} collective-permute-done((bf16[4,64,896]{2,1,0:T(8,128)(2,1)S(1)}, bf16[4,64,896]{2,1,0:T(8,128)(2,1)S(1)}, u32[]{:S(2)}, u32[]{:S(2)}) %collective-permute-start.3) | collective-permute-done | bytes 458784 | tf_op jit(solution)/shard_map/ppermute | solution.py:20
  126.1 11.8 %collective-permute-done.4 = bf16[4,64,896]{2,1,0:T(8,128)(2,1)S(1)} collective-permute-done((bf16[4,64,896]{2,1,0:T(8,128)(2,1)S(1)}, bf16[4,64,896]{2,1,0:T(8,128)(2,1)S(1)}, u32[]{:S(2)}, u32[]{:S(2)}) %collective-permute-start.4) | collective-permute-done | bytes 458784 | tf_op jit(solution)/shard_map/ppermute | solution.py:20
  138.7 11.3 %collective-permute-done.5 = bf16[4,64,896]{2,1,0:T(8,128)(2,1)} collective-permute-done((bf16[4,64,896]{2,1,0:T(8,128)(2,1)S(1)}, bf16[4,64,896]{2,1,0:T(8,128)(2,1)}, u32[]{:S(2)}, u32[]{:S(2)}) %collective-permute-start.5) | collective-permute-done | bytes 458784 | tf_op jit(solution)/shard_map/ppermute | solution.py:20
  150.2 2.2 copy.33
  152.4 9.1 %collective-permute-done.6 = bf16[4,64,896]{2,1,0:T(8,128)(2,1)} collective-permute-done((bf16[4,64,896]{2,1,0:T(8,128)(2,1)}, bf16[4,64,896]{2,1,0:T(8,128)(2,1)}, u32[]{:S(2)}, u32[]{:S(2)}) %collective-permute-start.6) | collective-permute-done | bytes 458784 | tf_op jit(solution)/shard_map/ppermute | solution.py:20
  163.7 1.1 constant_dynamic-update-slice_fusion.13
  170.1 3.0 %fusion.14 = bf16[16,64,896]{2,0,1:T(8,128)(2,1)S(1)} fusion(bf16[32,64,896]{2,1,0:T(8,128)(2,1)S(1)} %constant_dynamic-slice_fusion, s32[16]{0:T(128)S(1)} %add.38), kind=kOutput, calls=%fused_computation.18 | convolution fusion | flops 58720768 | bytes 5505088 | tf_op jit(solution)/shard_map/rb,bte->rte/dot_general | solution.py:64
  173.1 9.7 %convert_bitcast_fusion = bf16[2,16,64,2048]{3,2,0,1:T(8,128)(2,1)S(1)} fusion(bf16[2,896,2048]{2,1,0:T(8,128)(2,1)S(1)} %bitcast.110, bf16[16,64,896]{2,0,1:T(8,128)(2,1)S(1)} %fusion.14), kind=kOutput, calls=%fused_computation.2 | convolution fusion | flops 7520387072 | bytes 17563648 | tf_op jit(solution)/shard_map/rte,pef->prtf/dot_general | solution.py:67
  182.8 1.2 fusion.63
  184.0 1.4 copy.32
  185.4 3.0 %fusion.11 = f32[8,16,128,64]{2,3,1,0:T(8,128)S(1)} fusion(bf16[8,128,16,128]{3,2,1,0:T(8,128)(2,1)S(1)} %bitcast.103, bf16[8,64,16,128]{3,2,1,0:T(8,128)(2,1)S(1)} %bitcast.106), kind=kOutput, calls=%fused_computation.13 | convolution fusion | flops 268435456 | bytes 10485760 | tf_op jit(solution)/shard_map/cqhd,ckhd->chqk/dot_general | solution.py:74
  188.4 2.2 fusion.70
  190.6 3.3 %copy.34 = bf16[128,8,16,128]{3,2,1,0:T(8,128)(2,1)} copy(bf16[128,8,16,128]{3,1,2,0:T(8,128)(2,1)S(1)} %bitcast.104) | data formatting | bytes 8388608
  194.0 18.6 %convert_bitcast_fusion.1 = bf16[8,64,16,128]{3,1,2,0:T(8,128)(2,1)} fusion(bf16[8,128,16,128]{3,2,1,0:T(8,128)(2,1)} %bitcast.107, f32[8,16,64]{2,1,0:T(8,128)S(1)} %fusion.70, f32[8,16,128,64]{2,3,1,0:T(8,128)} %copy-done), kind=kOutput, calls=%fused_computation.21 | convolution fusion | flops 274735232 | bytes 10518528 | tf_op jit(solution)/shard_map/chqk,ckhd->cqhd/dot_general | solution.py:78
  212.6 3.0 %copy.25 = bf16[8,64,16,128]{3,2,1,0:T(8,128)(2,1)S(1)} copy(bf16[8,64,16,128]{3,1,2,0:T(8,128)(2,1)} %convert_bitcast_fusion.1) | data formatting | bytes 4194304 | tf_op jit(solution)/shard_map/convert_element_type | solution.py:80
  215.6 2.3 %reshape.44 = bf16[1,512,2048]{2,1,0:T(8,128)(2,1)} reshape(bf16[8,64,16,128]{3,2,1,0:T(8,128)(2,1)S(1)} %copy.25) | data formatting | bytes 4194304 | tf_op jit(solution)/shard_map/reshape | solution.py:81
  (60 shorter events, 13.5 us)
Async XLA Ops:
  6.5 52.2 %all-gather.2.cloned.1.call-start = ((), (), s32[]{:S(2)}) async-start(), calls=%async_computation | async-start | bytes 8028160 | tf_op jit(solution)/shard_map/all_gather | solution.py:55
  64.6 1.5 copy-start.7
  65.6 84.4 %copy-start.8 = (s32[1,8,2]{1,2,0:T(2,128)S(1)}, s32[1,8,2]{1,2,0:T(2,128)}, u32[]{:S(2)}) copy-start(s32[1,8,2]{1,2,0:T(2,128)} %param.10) | copy-start | bytes 196
  65.6 84.4 %copy-start.9 = (s32[1,8,2]{1,2,0:T(2,128)S(1)}, s32[1,8,2]{1,2,0:T(2,128)}, u32[]{:S(2)}) copy-start(s32[1,8,2]{1,2,0:T(2,128)} %param.9) | copy-start | bytes 196
  68.2 15.4 %collective-permute-start = (bf16[4,64,896]{2,1,0:T(8,128)(2,1)S(1)}, bf16[4,64,896]{2,1,0:T(8,128)(2,1)S(1)}, u32[]{:S(2)}, u32[]{:S(2)}) collective-permute-start(bf16[4,64,896]{2,1,0:T(8,128)(2,1)S(1)} %fusion.30), channel_id=1, source_target_pairs={{0,1},{1,2},{2,3},{3,4},{4,5},{5,6},{6,7},{7,0},{8,9},{9,10},{10,1... | collective-permute-start | bytes 1376264 | tf_op jit(solution)/shard_map/ppermute | solution.py:20
  83.6 14.6 %collective-permute-start.1 = (bf16[4,64,896]{2,1,0:T(8,128)(2,1)S(1)}, bf16[4,64,896]{2,1,0:T(8,128)(2,1)S(1)}, u32[]{:S(2)}, u32[]{:S(2)}) collective-permute-start(bf16[4,64,896]{2,1,0:T(8,128)(2,1)S(1)} %collective-permute-done), channel_id=1, source_target_pairs={{0,1},{1,2},{2,3},{3,4},{4,5},{5,6},{6,7},{7,0},{8,9},{9,10},{10,1... | collective-permute-start | bytes 1376264 | tf_op jit(solution)/shard_map/ppermute | solution.py:20
  98.2 13.7 %collective-permute-start.2 = (bf16[4,64,896]{2,1,0:T(8,128)(2,1)S(1)}, bf16[4,64,896]{2,1,0:T(8,128)(2,1)S(1)}, u32[]{:S(2)}, u32[]{:S(2)}) collective-permute-start(bf16[4,64,896]{2,1,0:T(8,128)(2,1)S(1)} %collective-permute-done.1), channel_id=1, source_target_pairs={{0,1},{1,2},{2,3},{3,4},{4,5},{5,6},{6,7},{7,0},{8,9},{9,10},{10,1... | collective-permute-start | bytes 1376264 | tf_op jit(solution)/shard_map/ppermute | solution.py:20
  111.9 0.8 copy-start.1
  112.6 12.7 %collective-permute-start.3 = (bf16[4,64,896]{2,1,0:T(8,128)(2,1)S(1)}, bf16[4,64,896]{2,1,0:T(8,128)(2,1)S(1)}, u32[]{:S(2)}, u32[]{:S(2)}) collective-permute-start(bf16[4,64,896]{2,1,0:T(8,128)(2,1)S(1)} %collective-permute-done.2), channel_id=1, source_target_pairs={{0,1},{1,2},{2,3},{3,4},{4,5},{5,6},{6,7},{7,0},{8,9},{9,10},{10,1... | collective-permute-start | bytes 1376264 | tf_op jit(solution)/shard_map/ppermute | solution.py:20
  125.4 0.8 copy-start.3
  126.1 11.8 %collective-permute-start.4 = (bf16[4,64,896]{2,1,0:T(8,128)(2,1)S(1)}, bf16[4,64,896]{2,1,0:T(8,128)(2,1)S(1)}, u32[]{:S(2)}, u32[]{:S(2)}) collective-permute-start(bf16[4,64,896]{2,1,0:T(8,128)(2,1)S(1)} %collective-permute-done.3), channel_id=1, source_target_pairs={{0,1},{1,2},{2,3},{3,4},{4,5},{5,6},{6,7},{7,0},{8,9},{9,10},{10,1... | collective-permute-start | bytes 1376264 | tf_op jit(solution)/shard_map/ppermute | solution.py:20
  137.9 0.8 copy-start.5
  138.7 11.3 %collective-permute-start.5 = (bf16[4,64,896]{2,1,0:T(8,128)(2,1)S(1)}, bf16[4,64,896]{2,1,0:T(8,128)(2,1)}, u32[]{:S(2)}, u32[]{:S(2)}) collective-permute-start(bf16[4,64,896]{2,1,0:T(8,128)(2,1)S(1)} %collective-permute-done.4), channel_id=1, source_target_pairs={{0,1},{1,2},{2,3},{3,4},{4,5},{5,6},{6,7},{7,0},{8,9},{9,10},{10,1... | collective-permute-start | bytes 1376264 | tf_op jit(solution)/shard_map/ppermute | solution.py:20
  150.0 11.5 %collective-permute-start.6 = (bf16[4,64,896]{2,1,0:T(8,128)(2,1)}, bf16[4,64,896]{2,1,0:T(8,128)(2,1)}, u32[]{:S(2)}, u32[]{:S(2)}) collective-permute-start(bf16[4,64,896]{2,1,0:T(8,128)(2,1)} %collective-permute-done.5), channel_id=1, source_target_pairs={{0,1},{1,2},{2,3},{3,4},{4,5},{5,6},{6,7},{7,0},{8,9},{9,10},{10,1... | collective-permute-start | bytes 1376264 | tf_op jit(solution)/shard_map/ppermute | solution.py:20
  162.5 6.8 %copy-start.6 = (bf16[4,64,896]{2,1,0:T(8,128)(2,1)S(1)}, bf16[4,64,896]{2,1,0:T(8,128)(2,1)}, u32[]{:S(2)}) copy-start(bf16[4,64,896]{2,1,0:T(8,128)(2,1)} %copy-done.5) | copy-start | bytes 1376260
  163.7 5.7 %copy-start.4 = (bf16[4,64,896]{2,1,0:T(8,128)(2,1)S(1)}, bf16[4,64,896]{2,1,0:T(8,128)(2,1)}, u32[]{:S(2)}) copy-start(bf16[4,64,896]{2,1,0:T(8,128)(2,1)} %copy-done.3) | copy-start | bytes 1376260
  164.8 4.7 %copy-start.2 = (bf16[4,64,896]{2,1,0:T(8,128)(2,1)S(1)}, bf16[4,64,896]{2,1,0:T(8,128)(2,1)}, u32[]{:S(2)}) copy-start(bf16[4,64,896]{2,1,0:T(8,128)(2,1)} %copy-done.1) | copy-start | bytes 1376260
  169.7 3.4 %slice-start = ((s8[7340032]{0:T(1024)(128)(4,1)}), s8[4194304]{0:T(1024)(128)(4,1)S(1)}, s32[]{:S(2)}) async-start(s8[7340032]{0:T(1024)(128)(4,1)} %bitcast.109), calls=%async_computation.1 | async-start | bytes 8388608
  169.7 3.3 %slice-start.1 = ((s8[7340032]{0:T(1024)(128)(4,1)}), s8[3145728]{0:T(1024)(128)(4,1)S(1)}, s32[]{:S(2)}) async-start(s8[7340032]{0:T(1024)(128)(4,1)} %bitcast.109), calls=%async_computation.2 | async-start | bytes 6291456
  188.4 5.6 %copy-start = (f32[8,16,128,64]{2,3,1,0:T(8,128)}, f32[8,16,128,64]{2,3,1,0:T(8,128)S(1)}, u32[]{:S(2)}) copy-start(f32[8,16,128,64]{2,3,1,0:T(8,128)S(1)} %fusion.11) | copy-start | bytes 12582916
Sparse Core Ops, SparseCore 0:
  8.9 49.8 all-gather.1
